TPU v7x, 512 devices: a whole 4x8x8 slice. The times are simulated.
512 devices in a mesh: freq: 8 (over x, core), geo: 64 (over z, y).
Axes of the slice: x: 4, y: 8, z: 8, core: 2. Of those that a mesh axis runs over, the one named last changes fastest.
Arguments:
- energy: float32 [256, 48, 36, 128], P('geo', 'freq'), may hold values from 0.1 to 1.5
- water_depth: float32 [256, 128], P('geo'), may hold values from 0.5 to 4
- wet_mask: int32 [256, 128], P('geo'), may hold values 0 or 1
- vegetation: int32 [256, 128], P('geo'), may hold values 0 or 1
- canopy: float32 [256, 128], P('geo'), may hold values from 0.004 to 0.04
- quad_offsets: int32 [4], replicated, may hold values from 1 to 3, as said below
- quad_weights: float32 [2], replicated, may hold values from 0.2 to 0.8
Outputs:
- energy_next: float32 [256, 48, 36, 128], P('geo', 'freq')
- orbital: float32 [256, 128], P('geo')
Inputs may be any that keep to these rules, and one draw needn't show every extreme that they name: `quad_offsets`: offsets a and the two direction turns lie in 1 .. 3; the lower frequency offset b equals 3 in every draw.
All inputs are finite; a program needn't handle non-finite values. No bound on the sum of `wet_mask` or of `vegetation` on one device may be relied on, other than what follows from the above.
Results may differ from a plain program's by a relative error of at most 0.00002.
Values sent between devices are 32-bit elements; how exact they have to be, the bound alone decides.
No kernel may reach another device: no remote copies, remote signals or barrier semaphores. Data moves between devices by JAX's collectives and lax.ppermute only.
A program may use at most 64 MiB of HBM per device.

v0:
```python
import math
import jax
import jax.numpy as jnp
from jax import lax
from jax.sharding import PartitionSpec as P

FH = 4
SUBSTEPS = 8
gravity = 9.81
base_freq = 0.03
freq_ratio = 1.05
cell_size = 20.0
sub_step = 2.0
coupling = 0.01
coef_plus = 0.4096
coef_minus = 3.1605
coef_both = 2.589


def from_neighbour(block, axis, distance, cyclic=False):
    count = lax.axis_size(axis)
    if cyclic:
        pairs = [(i, (i + distance) % count) for i in range(count)]
    else:
        pairs = [(i, i + distance) for i in range(count) if 0 <= i + distance < count]
    return lax.ppermute(block, axis, pairs)


def halo(block, axis, dim, width, side, cyclic=False):
    size = block.shape[dim]
    parts = []
    distance = 1
    need = width
    while need > 0:
        take = min(size, need)
        if side < 0:
            piece = lax.slice_in_dim(block, size - take, size, axis=dim)
            parts.insert(0, from_neighbour(piece, axis, distance, cyclic))
        else:
            piece = lax.slice_in_dim(block, 0, take, axis=dim)
            parts.append(from_neighbour(piece, axis, -distance, cyclic))
        need -= take
        distance += 1
    return parts


def butterfly_sum(value, axis):
    count = lax.axis_size(axis)
    assert count & count - 1 == 0
    step = 1
    while step < count:
        value = value + lax.ppermute(value, axis, [(i, i ^ step) for i in range(count)])
        step *= 2
    return value


def gathered_sum(known, index, count, value):
    reach = max(known)
    if count > 2 * (2 * reach + 1) - 2 or count % 2:
        return butterfly_sum(value, "freq")
    far = count // 2
    ordered = jnp.stack([known[o] for o in range(-reach, reach + 1)])
    more = from_neighbour(ordered, "freq", far, True)
    table = []
    for rel in range(count):
        off = rel if rel <= reach else rel - count
        if -reach <= off <= reach:
            table.append(known[off])
        else:
            table.append(more[rel - far + reach])
    table = jnp.stack(table)
    table = jnp.concatenate([table, table], axis=0)
    start = (count - index) % count
    glob = lax.dynamic_slice_in_dim(table, start, count, axis=0)
    while glob.shape[0] > 1:
        glob = glob[0::2] + glob[1::2]
    return glob[0]


def physics(radian_freq, water_depth, dir_count):
    square = (radian_freq * radian_freq)[None, :, None]
    column = water_depth[:, None, :]
    depth_ratio = square * column / gravity
    depth_wave = depth_ratio / jnp.sqrt(jnp.tanh(depth_ratio))
    group_speed = (
        radian_freq[None, :, None]
        * column
        / depth_wave
        * (0.5 + depth_wave / jnp.sinh(2.0 * depth_wave))
    )
    orbit_weight = (
        square
        / jnp.sinh(depth_wave) ** 2
        * (radian_freq * (freq_ratio - 1.0))[None, :, None]
        * (2.0 * math.pi / dir_count)
    )
    return (group_speed, orbit_weight)


def angles_of(dir_count):
    angles = (jnp.arange(dir_count, dtype=jnp.float32) + 0.5) * (2.0 * math.pi / dir_count)
    return (jnp.cos(angles), jnp.sin(angles))


def shifted(doubled, freq_start, dir_off, count):
    dir_count = doubled.shape[2] // 2
    starts = (jnp.zeros((), jnp.int32), freq_start, dir_off % dir_count, jnp.zeros((), jnp.int32))
    return lax.dynamic_slice(
        doubled, starts, (doubled.shape[0], count, dir_count, doubled.shape[3])
    )


def source_change(extended, quad_offsets, quad_weights, count):
    up_bins, down_bins, up_turn, down_turn = (
        quad_offsets[0],
        quad_offsets[1],
        quad_offsets[2],
        quad_offsets[3],
    )
    weight_up, weight_down = (quad_weights[0], quad_weights[1])
    wide = count + 2 * FH
    doubled = jnp.concatenate([extended, extended], axis=2)
    centre = lax.slice_in_dim(extended, FH, FH + wide, axis=1)
    upper = weight_up * shifted(doubled, FH + up_bins, up_turn, wide) + (1.0 - weight_up) * shifted(
        doubled, FH + up_bins + 1, up_turn, wide
    )
    lower = weight_down * shifted(doubled, FH - down_bins, -down_turn, wide) + (
        1.0 - weight_down
    ) * shifted(doubled, FH - down_bins - 1, -down_turn, wide)
    transfer = coupling * (
        centre * centre * (coef_plus * upper + coef_minus * lower)
        - coef_both * centre * upper * lower
    )
    spread = jnp.concatenate([transfer, transfer], axis=2)
    gained = weight_up * shifted(spread, FH - up_bins, -up_turn, count) + (
        1.0 - weight_up
    ) * shifted(spread, FH - up_bins - 1, -up_turn, count)
    gained = (
        gained
        + weight_down * shifted(spread, FH + down_bins, down_turn, count)
        + (1.0 - weight_down) * shifted(spread, FH + down_bins + 1, down_turn, count)
    )
    own = lax.slice_in_dim(transfer, FH, FH + count, axis=1)
    return gained - 2.0 * own


def east_west(east_flux, cosines):
    zeros = jnp.zeros_like(east_flux[..., :1])
    behind = jnp.concatenate([zeros, east_flux[..., :-1]], axis=-1)
    ahead = jnp.concatenate([east_flux[..., 1:], zeros], axis=-1)
    east_going = (cosines > 0.0)[None, None, :, None]
    return jnp.where(east_going, east_flux - behind, ahead - east_flux)


def propagate(spectrum, speed, wet, cosines, sines, northward):
    step_ratio = sub_step / cell_size
    east_speed = speed[:, :, None, :] * cosines[None, None, :, None]
    north_speed = speed[:, :, None, :] * sines[None, None, :, None]
    rows = spectrum.shape[0]
    for substep in range(SUBSTEPS):
        lo, hi = (substep, rows) if northward else (0, rows - substep)
        east_flux = east_speed[lo:hi] * spectrum
        north_flux = north_speed[lo:hi] * spectrum
        along = north_flux[1:] - north_flux[:-1]
        across = east_west(east_flux, cosines)
        if northward:
            spectrum = wet[lo + 1 : hi, None, None, :] * (
                spectrum[1:] - step_ratio * (across[1:] + along)
            )
        else:
            spectrum = wet[lo : hi - 1, None, None, :] * (
                spectrum[:-1] - step_ratio * (across[:-1] + along)
            )
    return spectrum


def body(energy, water_depth, wet_mask, vegetation, canopy, quad_offsets, quad_weights):
    tile_rows, freq_count, dir_count, tile_cols = energy.shape
    wet_field = wet_mask.astype(jnp.float32)
    veg_field = vegetation.astype(jnp.float32)
    wet_four = wet_field[:, None, None, :]
    masked = wet_four * energy
    first_bin = lax.axis_index("freq") * freq_count
    bin_index = (first_bin + jnp.arange(freq_count, dtype=jnp.int32)).astype(jnp.float32)
    radian_freq = 2.0 * math.pi * base_freq * jnp.power(freq_ratio, bin_index)
    half = dir_count // 2
    cosines, sines = angles_of(dir_count)
    fields = jnp.zeros((tile_rows, 1, half, tile_cols), jnp.float32)
    fields = fields.at[:, 0, 0, :].set(wet_field).at[:, 0, 1, :].set(water_depth)
    north_msg = jnp.concatenate([masked[:, :, :half], fields], axis=1)
    south_msg = jnp.concatenate([masked[:, :, half:], fields], axis=1)
    below = halo(north_msg, "geo", 0, SUBSTEPS, -1)
    above = halo(south_msg, "geo", 0, SUBSTEPS, +1)
    group_speed, orbit_weight = physics(radian_freq, water_depth, dir_count)
    partial_value = jnp.sum(orbit_weight * jnp.sum(energy, axis=2), axis=1)
    freq_index = lax.axis_index("freq")
    freq_total = lax.axis_size("freq")
    slot = jnp.zeros((tile_rows, 1, dir_count, tile_cols), jnp.float32)
    slot = slot.at[:, 0, 0, :].set(partial_value)
    gathered = lax.all_gather(jnp.concatenate([masked, slot], axis=1), "freq", axis=1, tiled=True)
    gathered = gathered.reshape(tile_rows, freq_total, freq_count + 1, dir_count, tile_cols)
    partials = gathered[:, :, freq_count, 0, :]
    spectrum_all = gathered[:, :, :freq_count].reshape(
        tile_rows, freq_total * freq_count, dir_count, tile_cols
    )
    padded_all = jnp.pad(spectrum_all, ((0, 0), (2 * FH, 2 * FH), (0, 0), (0, 0)))
    extended = lax.dynamic_slice_in_dim(padded_all, first_bin, freq_count + 4 * FH, axis=1)
    glob = jnp.moveaxis(partials, 1, 0)
    while glob.shape[0] > 1:
        glob = glob[0::2] + glob[1::2]
    orbital = jnp.sqrt(glob[0])
    full_step = SUBSTEPS * sub_step
    damping = 1.0 + full_step * canopy * veg_field * orbital
    change = source_change(extended, quad_offsets, quad_weights, freq_count)
    increment = (masked + full_step * change) / damping[:, None, None, :] - masked
    geo_index = lax.axis_index("geo")
    geo_count = lax.axis_size("geo")

    def unpack(parts, offsets):
        spectra, speeds, wets = ([], [], [])
        for part, offset in zip(parts, offsets):
            valid = (geo_index + offset >= 0) & (geo_index + offset < geo_count)
            depth = jnp.where(valid, part[:, freq_count, 1, :], 1.0)
            spectra.append(part[:, :freq_count])
            wets.append(part[:, freq_count, 0, :])
            speeds.append(physics(radian_freq, depth, dir_count)[0])
        return (spectra, speeds, wets)

    n_off = [-(len(below) - k) for k in range(len(below))]
    b_spec, b_speed, b_wet = unpack(below, n_off)
    north = propagate(
        jnp.concatenate(b_spec + [masked[:, :, :half]], axis=0),
        jnp.concatenate(b_speed + [group_speed], axis=0),
        jnp.concatenate(b_wet + [wet_field], axis=0),
        cosines[:half],
        sines[:half],
        True,
    )
    s_off = [k + 1 for k in range(len(above))]
    a_spec, a_speed, a_wet = unpack(above, s_off)
    south = propagate(
        jnp.concatenate([masked[:, :, half:]] + a_spec, axis=0),
        jnp.concatenate([group_speed] + a_speed, axis=0),
        jnp.concatenate([wet_field] + a_wet, axis=0),
        cosines[half:],
        sines[half:],
        False,
    )
    moved = jnp.concatenate([north, south], axis=2)
    return (wet_four * (moved + increment), orbital)


def solution(mesh):
    placed = (
        P("geo", "freq", None, None),
        P("geo", None),
        P("geo", None),
        P("geo", None),
        P("geo", None),
        P(),
        P(),
    )
    return jax.shard_map(
        body,
        mesh=mesh,
        in_specs=placed,
        out_specs=(P("geo", "freq", None, None), P("geo", None)),
        check_vma=False,
    )
```

profile of v0, /device:TPU:1, one launch (start us, length us, event | category | flops | bytes accessed | tf_op | source)
XLA Modules:
  0.0 115.2 jit_solution(11909362313528127280)
XLA Ops:
  7.2 0.7 fusion.169
  7.9 1.1 fusion.159
  9.7 1.3 %constant_dynamic-update-slice_fusion = f32[4,1,18,128]{3,0,2,1:T(4,128)S(1)} fusion(f32[4,1,18,128]{3,0,2,1:T(4,128)S(1)} %scatter.10, s32[]{:T(128)} %bitcast.2, f32[4,128]{1,0:T(4,128)} %param.14), kind=kLoop, calls=%fused_computation.258 | loop fusion | bytes 4100 | tf_op jit(solution)/shard_map/scatter | solution.py:189
  11.1 1.3 %collective-permute-start.2 = (f32[4,7,18,128]{3,0,2,1:T(4,128)S(1)}, f32[4,7,18,128]{3,0,2,1:T(4,128)S(1)}, u32[]{:S(2)}, u32[]{:S(2)}) collective-permute-start(f32[4,7,18,128]{3,0,2,1:T(4,128)S(1)} %get-tuple-element.123), channel_id=1, source_target_pairs={{1,0},{2,1},{3,2},{4,3},{5,4},{6,5},{7,6},{8,7},{9,8},{10,9},{11,1... | collective-permute-start | bytes 774152 | tf_op jit(solution)/shard_map/ppermute | solution.py:26
  12.4 1.3 %collective-permute-start.3 = (f32[4,7,18,128]{3,0,2,1:T(4,128)S(1)}, f32[4,7,18,128]{3,0,2,1:T(4,128)S(1)}, u32[]{:S(2)}, u32[]{:S(2)}) collective-permute-start(f32[4,7,18,128]{3,0,2,1:T(4,128)S(1)} %get-tuple-element.123), channel_id=1, source_target_pairs={{2,0},{3,1},{4,2},{5,3},{6,4},{7,5},{8,6},{9,7},{10,8},{11,9},{12,... | collective-permute-start | bytes 774152 | tf_op jit(solution)/shard_map/ppermute | solution.py:26
  13.7 6.5 %collective-permute-start.1 = (f32[4,7,18,128]{3,0,2,1:T(4,128)S(1)}, f32[4,7,18,128]{3,0,2,1:T(4,128)S(1)}, u32[]{:S(2)}, u32[]{:S(2)}) collective-permute-start(f32[4,7,18,128]{3,0,2,1:T(4,128)S(1)} %get-tuple-element.122), channel_id=1, source_target_pairs={{0,2},{1,3},{2,4},{3,5},{4,6},{5,7},{6,8},{7,9},{8,10},{9,11},{10,... | collective-permute-start | bytes 774152 | tf_op jit(solution)/shard_map/ppermute | solution.py:26
  20.2 3.2 %collective-permute-start = (f32[4,7,18,128]{3,0,2,1:T(4,128)S(1)}, f32[4,7,18,128]{3,0,2,1:T(4,128)S(1)}, u32[]{:S(2)}, u32[]{:S(2)}) collective-permute-start(f32[4,7,18,128]{3,0,2,1:T(4,128)S(1)} %get-tuple-element.122), channel_id=1, source_target_pairs={{0,1},{1,2},{2,3},{3,4},{4,5},{5,6},{6,7},{7,8},{8,9},{9,10},{10,1... | collective-permute-start | bytes 774152 | tf_op jit(solution)/shard_map/ppermute | solution.py:26
  24.1 1.3 %fusion.170 = (f32[1]{0:T(128)}, f32[1]{0:T(128)}) fusion(f32[2]{0:T(128)} %param.19), kind=kLoop, calls=%fused_computation.307 | loop fusion | bytes 16 | tf_op jit(solution)/shard_map/slice | solution.py:120
  25.4 1.5 %fusion.171 = (s32[1]{0:T(128)}, s32[1]{0:T(128)}, s32[1]{0:T(128)}, s32[1]{0:T(128)}) fusion(s32[4]{0:T(128)} %param.18), kind=kLoop, calls=%fused_computation.308 | loop fusion | bytes 32 | tf_op jit(solution)/shard_map/slice | solution.py:117
  40.5 0.6 slice.815
  44.1 1.0 multiply_reduce_fusion
  45.1 0.6 pad_maximum_fusion.4
  51.9 0.9 select_maximum_fusion
  52.8 1.0 slice.817
  53.8 1.2 %fusion.94 = (f32[12,6,18,128]{3,0,2,1:T(8,128)S(1)}, f32[12,6,18,128]{3,0,2,1:T(8,128)S(1)}, f32[12,6,18,128]{3,0,2,1:T(8,128)S(1)}, f32[12,6,18,128]{3,0,2,1:T(8,128)S(1)}, f32[12,6,18,128]{3,0,2,1:T(8,128)S(1)}) fusion(f32[18]{0:T(128)} %get-tuple-element.155, f32[12,6,128]{2,0,1:T(8,128)} %get-tuple-element.124, ...), kind=kLoop, calls=%fused_computation.195 | loop fusion | flops 995328 | bytes 4018320 | tf_op jit(solution)/shard_map/mul | solution.py:162
  55.4 0.8 slice_multiply_fusion.11
  56.8 0.8 slice_multiply_fusion.9
  58.3 0.8 slice_multiply_fusion.7
  62.5 0.6 fusion.106
  63.2 34.5 %all-gather.2.cloned.1.call-done = f32[4,56,36,128]{3,0,2,1:T(4,128)} async-done(((f32[4,7,36,128]{3,0,2,1:T(4,128)}), f32[4,56,36,128]{3,0,2,1:T(4,128)}) %all-gather.2.cloned.1.call-update) | async-done | bytes 4128784 | tf_op jit(solution)/shard_map/all_gather | solution.py:200
  97.6 2.2 %slice.954 = f32[4,8,6,36,128]{4,0,3,2,1:T(4,128)S(1)} slice(f32[4,8,7,36,128]{4,0,3,2,1:T(4,128)} %bitcast.61), slice={[0:4], [0:8], [0:6], [0:36], [0:128]} | slice | bytes 7077888 | tf_op jit(solution)/shard_map/slice | solution.py:203
  99.9 0.7 slice_bitcast_fusion
  101.6 3.8 %subtract_multiply_fusion = f32[4,14,36,128]{3,0,2,1:T(4,128)S(1)} fusion(s32[]{:T(128)S(6)} %select_n.216, s32[]{:T(128)S(6)} %select_n.215, f32[4,22,36,128]{3,0,2,1:T(4,128)S(1)} %pad_dynamic-slice_fusion.1, s32[]{:T(128)S(6)} %select_n.213, s32[]{:T(128)S(6)} %select_n.212, s32[]{:T(128)S(6)} %select_n.211, s32[]{:T(128)S(6)} %select_n.209, ...), kind=kLoop, calls=%fused_computation.28 | loop fusion | flops 5160960 | bytes 6193196 | tf_op jit(solution)/shard_map/mul | solution.py:130
  105.4 3.0 %fusion.93 = f32[4,6,36,128]{3,0,2,1:T(4,128)} fusion(f32[4,6,18,128]{3,0,2,1:T(4,128)S(1)} %get-tuple-element.129, f32[4,6,18,128]{3,0,2,1:T(4,128)S(1)} %get-tuple-element.128, f32[4,14,36,128]{3,0,2,1:T(4,128)S(1)} %subtract_multiply_fusion, s32[]{:T(128)S(6)} %select_n.224, s32[]{:T(128)S(6)} %select_n.223, s32[]{:T(128)S(6)} %select_n.221, ...), kind=kLoop, calls=%fused_computation.192 | loop fusion | flops 2322432 | bytes 2805800 | tf_op jit(solution)/shard_map/mul | solution.py:250
  (100 shorter events, 16.6 us)
Async XLA Ops:
  7.2 90.5 %all-gather.2.cloned.1.call-start = ((), (), s32[]{:S(2)}) async-start(), calls=%async_computation | async-start | bytes 4644864 | tf_op jit(solution)/shard_map/all_gather | solution.py:200
  11.1 29.2 %collective-permute-start.2 = (f32[4,7,18,128]{3,0,2,1:T(4,128)S(1)}, f32[4,7,18,128]{3,0,2,1:T(4,128)S(1)}, u32[]{:S(2)}, u32[]{:S(2)}) collective-permute-start(f32[4,7,18,128]{3,0,2,1:T(4,128)S(1)} %get-tuple-element.123), channel_id=1, source_target_pairs={{1,0},{2,1},{3,2},{4,3},{5,4},{6,5},{7,6},{8,7},{9,8},{10,9},{11,1... | collective-permute-start | bytes 774152 | tf_op jit(solution)/shard_map/ppermute | solution.py:26
  12.4 28.0 %collective-permute-start.3 = (f32[4,7,18,128]{3,0,2,1:T(4,128)S(1)}, f32[4,7,18,128]{3,0,2,1:T(4,128)S(1)}, u32[]{:S(2)}, u32[]{:S(2)}) collective-permute-start(f32[4,7,18,128]{3,0,2,1:T(4,128)S(1)} %get-tuple-element.123), channel_id=1, source_target_pairs={{2,0},{3,1},{4,2},{5,3},{6,4},{7,5},{8,6},{9,7},{10,8},{11,9},{12,... | collective-permute-start | bytes 774152 | tf_op jit(solution)/shard_map/ppermute | solution.py:26
  13.7 26.7 %collective-permute-start.1 = (f32[4,7,18,128]{3,0,2,1:T(4,128)S(1)}, f32[4,7,18,128]{3,0,2,1:T(4,128)S(1)}, u32[]{:S(2)}, u32[]{:S(2)}) collective-permute-start(f32[4,7,18,128]{3,0,2,1:T(4,128)S(1)} %get-tuple-element.122), channel_id=1, source_target_pairs={{0,2},{1,3},{2,4},{3,5},{4,6},{5,7},{6,8},{7,9},{8,10},{9,11},{10,... | collective-permute-start | bytes 774152 | tf_op jit(solution)/shard_map/ppermute | solution.py:26
  20.2 20.2 %collective-permute-start = (f32[4,7,18,128]{3,0,2,1:T(4,128)S(1)}, f32[4,7,18,128]{3,0,2,1:T(4,128)S(1)}, u32[]{:S(2)}, u32[]{:S(2)}) collective-permute-start(f32[4,7,18,128]{3,0,2,1:T(4,128)S(1)} %get-tuple-element.122), channel_id=1, source_target_pairs={{0,1},{1,2},{2,3},{3,4},{4,5},{5,6},{6,7},{7,8},{8,9},{9,10},{10,1... | collective-permute-start | bytes 774152 | tf_op jit(solution)/shard_map/ppermute | solution.py:26
  40.4 5.4 %copy-start.2 = (f32[4,7,18,128]{3,0,2,1:T(4,128)}, f32[4,7,18,128]{3,0,2,1:T(4,128)S(1)}, u32[]{:S(2)}) copy-start(f32[4,7,18,128]{3,0,2,1:T(4,128)S(1)} %collective-permute-done) | copy-start | bytes 774148
  40.4 6.1 %copy-start.1 = (f32[4,7,18,128]{3,0,2,1:T(4,128)}, f32[4,7,18,128]{3,0,2,1:T(4,128)S(1)}, u32[]{:S(2)}) copy-start(f32[4,7,18,128]{3,0,2,1:T(4,128)S(1)} %collective-permute-done.1) | copy-start | bytes 774148
  51.7 2.1 %slice-start = ((f32[4,7,18,128]{3,0,2,1:T(4,128)}), f32[4,6,18,128]{3,0,2,1:T(4,128)S(1)}, s32[]{:S(2)}) async-start(f32[4,7,18,128]{3,0,2,1:T(4,128)} %copy-done.1), calls=%async_computation.1 | async-start | bytes 442368 | tf_op jit(solution)/shard_map/slice | solution.py:224
  53.8 1.6 %copy-start.5 = (f32[11,128]{1,0:T(8,128)S(1)}, f32[11,128]{1,0:T(8,128)}, u32[]{:S(2)}) copy-start(f32[11,128]{1,0:T(8,128)} %slice.815) | copy-start | bytes 16900
  56.1 0.7 copy-start.4
  57.6 0.7 copy-start.3
  59.5 0.8 copy-start.8
  60.3 0.7 copy-start.7
  61.0 0.9 copy-start.6
  99.9 1.1 copy-start.9
  99.9 1.1 copy-start.10
  101.0 4.4 %copy-start = (f32[4,6,36,128]{3,0,2,1:T(4,128)S(1)}, f32[4,6,36,128]{3,0,2,1:T(4,128)}, u32[]{:S(2)}) copy-start(f32[4,6,36,128]{3,0,2,1:T(4,128)} %param.13) | copy-start | bytes 1327108
Sparse Core Ops, SparseCore 0:
  52.9 44.6 all-gather.1
where the time goes:
time: 116 us; the launch traced here: 115 us
  waiting for transfers between devices  34.5 us (30%)
  between operations  28 us (24%)
  other arithmetic  22.8 us (20%)
  local copies, waits for them, and re-layouts  17.7 us (15%)
  starting transfers between devices  12.3 us (11%)
    all_gather x1, waiting for transfers between devices, body(): lax.all_gather(jnp.concatenate([masked, slot], axis=1), 'freq', axis=1, t...  34.5 us
    ppermute x4, starting transfers between devices, from_neighbour(): return lax.ppermute(block, axis, pairs)  12.3 us
    mul x16, other arithmetic, propagate(): east_flux = east_speed[lo:hi] * spectrum  8.76 us
    slice x16, local copies, waits for them, and re-layouts, east_west(): behind = jnp.concatenate([zeros, east_flux[..., :-1]], axis=-1)  3.96 us
    mul x1, other arithmetic, source_change(): coupling * (centre * centre * (coef_plus * upper + coef_minus * lower) -...  3.76 us
    slice x6, local copies, waits for them, and re-layouts, propagate(): wet[lo + 1:hi, None, None, :]  3.61 us
    mul x1, other arithmetic, body(): return (wet_four * (moved + increment), orbital)  3.01 us
  transfers between devices with their start and end apart: 5, of which 1 were waited for; matrix products, arithmetic and copies ran while one was open for 11% of the time, Pallas kernels for 0%

commit v1 on v0

--- a/solution.py
+++ b/solution.py
@@ -15,6 +15,19 @@
 coef_plus = 0.4096
 coef_minus = 3.1605
 coef_both = 2.589
+
+
+def ring_gather(value, axis, dim):
+    ways = lax.axis_size(axis)
+    up = [(d, (d + 1) % ways) for d in range(ways)]
+    down = [(d, (d - 1) % ways) for d in range(ways)]
+    earlier, later = ([value], [value])
+    for _ in range(ways // 2):
+        earlier.append(lax.ppermute(earlier[-1], axis, up))
+    for _ in range((ways - 1) // 2):
+        later.append(lax.ppermute(later[-1], axis, down))
+    line = jnp.concatenate([*earlier[::-1], *later[1:]], axis=dim)
+    return jnp.roll(line, (lax.axis_index(axis) - ways // 2) * value.shape[dim], axis=dim)
 
 
 def from_neighbour(block, axis, distance, cyclic=False):
@@ -197,7 +210,7 @@
     freq_total = lax.axis_size("freq")
     slot = jnp.zeros((tile_rows, 1, dir_count, tile_cols), jnp.float32)
     slot = slot.at[:, 0, 0, :].set(partial_value)
-    gathered = lax.all_gather(jnp.concatenate([masked, slot], axis=1), "freq", axis=1, tiled=True)
+    gathered = ring_gather(jnp.concatenate([masked, slot], axis=1), "freq", 1)
     gathered = gathered.reshape(tile_rows, freq_total, freq_count + 1, dir_count, tile_cols)
     partials = gathered[:, :, freq_count, 0, :]
     spectrum_all = gathered[:, :, :freq_count].reshape(

time: 116 us -> 96.5 us (0.83)
  the two profiles are of different devices: /device:TPU:1 before, /device:TPU:7 now
where the time goes in v1:
time: 96.5 us; the launch traced here: 95.9 us
  starting transfers between devices  29.1 us (30%)
  other arithmetic  20.5 us (21%)
  waiting for transfers between devices  20.4 us (21%)
  between operations  14.9 us (15%)
  local copies, waits for them, and re-layouts  10.9 us (11%)
    ppermute x4, starting transfers between devices, ring_gather(): earlier.append(lax.ppermute(earlier[-1], axis, up))  17.6 us
    ppermute x4, waiting for transfers between devices, ring_gather(): earlier.append(lax.ppermute(earlier[-1], axis, up))  16.4 us
    ppermute x4, starting transfers between devices, from_neighbour(): return lax.ppermute(block, axis, pairs)  11.5 us
    mul x16, other arithmetic, propagate(): east_flux = east_speed[lo:hi] * spectrum  7.69 us
    ppermute x3, waiting for transfers between devices, ring_gather(): later.append(lax.ppermute(later[-1], axis, down))  3.98 us
    slice x16, local copies, waits for them, and re-layouts, east_west(): behind = jnp.concatenate([zeros, east_flux[..., :-1]], axis=-1)  3.95 us
    mul x1, other arithmetic, source_change(): coupling * (centre * centre * (coef_plus * upper + coef_minus * lower) -...  3.94 us
    mul x1, other arithmetic, body(): return (wet_four * (moved + increment), orbital)  3.17 us
  transfers between devices with their start and end apart: 11, of which 4 were waited for; matrix products, arithmetic and copies ran while one was open for 18% of the time, Pallas kernels for 0%

profile of v1, /device:TPU:7, one launch (start us, length us, event | category | flops | bytes accessed | tf_op | source)
XLA Modules:
  0.0 95.9 jit_solution(4472078136862810695)
XLA Ops:
  0.6 0.7 convert_bitcast_fusion
  1.9 1.1 %fusion.159 = (f32[4,6,128]{2,0,1:T(4,128)S(1)}, f32[4,6,36,128]{3,0,2,1:T(4,128)S(1)}) fusion(f32[4,6,36,128]{3,0,2,1:T(4,128)} %param.13, f32[4,128]{1,0:T(4,128)S(1)} %get-tuple-element.135), kind=kLoop, calls=%fused_computation.314 | loop fusion | flops 218112 | bytes 899072 | tf_op jit(solution)/shard_map/reduce_sum | solution.py:208
  3.1 1.3 %constant_dynamic-update-slice_fusion.16 = f32[4,1,18,128]{3,0,2,1:T(4,128)S(1)} fusion(f32[4,1,18,128]{3,0,2,1:T(4,128)S(1)} %scatter.10, s32[]{:T(128)} %bitcast.2, f32[4,128]{1,0:T(4,128)} %param.14), kind=kLoop, calls=%fused_computation.276 | loop fusion | bytes 4100 | tf_op jit(solution)/shard_map/scatter | solution.py:202
  4.5 1.3 %collective-permute-start.2 = (f32[4,7,18,128]{3,0,2,1:T(4,128)S(1)}, f32[4,7,18,128]{3,0,2,1:T(4,128)S(1)}, u32[]{:S(2)}, u32[]{:S(2)}) collective-permute-start(f32[4,7,18,128]{3,0,2,1:T(4,128)S(1)} %get-tuple-element.123), channel_id=1, source_target_pairs={{1,0},{2,1},{3,2},{4,3},{5,4},{6,5},{7,6},{8,7},{9,8},{10,9},{11,1... | collective-permute-start | bytes 774152 | tf_op jit(solution)/shard_map/ppermute | solution.py:39
  5.8 1.3 %collective-permute-start.3 = (f32[4,7,18,128]{3,0,2,1:T(4,128)S(1)}, f32[4,7,18,128]{3,0,2,1:T(4,128)S(1)}, u32[]{:S(2)}, u32[]{:S(2)}) collective-permute-start(f32[4,7,18,128]{3,0,2,1:T(4,128)S(1)} %get-tuple-element.123), channel_id=1, source_target_pairs={{2,0},{3,1},{4,2},{5,3},{6,4},{7,5},{8,6},{9,7},{10,8},{11,9},{12,... | collective-permute-start | bytes 774152 | tf_op jit(solution)/shard_map/ppermute | solution.py:39
  7.1 4.0 %collective-permute-start = (f32[4,7,18,128]{3,0,2,1:T(4,128)S(1)}, f32[4,7,18,128]{3,0,2,1:T(4,128)S(1)}, u32[]{:S(2)}, u32[]{:S(2)}) collective-permute-start(f32[4,7,18,128]{3,0,2,1:T(4,128)S(1)} %get-tuple-element.122), channel_id=1, source_target_pairs={{0,1},{1,2},{2,3},{3,4},{4,5},{5,6},{6,7},{7,8},{8,9},{9,10},{10,1... | collective-permute-start | bytes 774152 | tf_op jit(solution)/shard_map/ppermute | solution.py:39
  11.1 4.9 %collective-permute-start.1 = (f32[4,7,18,128]{3,0,2,1:T(4,128)S(1)}, f32[4,7,18,128]{3,0,2,1:T(4,128)S(1)}, u32[]{:S(2)}, u32[]{:S(2)}) collective-permute-start(f32[4,7,18,128]{3,0,2,1:T(4,128)S(1)} %get-tuple-element.122), channel_id=1, source_target_pairs={{0,2},{1,3},{2,4},{3,5},{4,6},{5,7},{6,8},{7,9},{8,10},{9,11},{10,... | collective-permute-start | bytes 774152 | tf_op jit(solution)/shard_map/ppermute | solution.py:39
  16.3 1.4 %fusion.169 = (f32[1]{0:T(128)}, f32[1]{0:T(128)}) fusion(f32[2]{0:T(128)} %param.19), kind=kLoop, calls=%fused_computation.324 | loop fusion | bytes 16 | tf_op jit(solution)/shard_map/slice | solution.py:133
  17.7 1.5 %fusion.170 = (s32[1]{0:T(128)}, s32[1]{0:T(128)}, s32[1]{0:T(128)}, s32[1]{0:T(128)}) fusion(s32[4]{0:T(128)} %param.18), kind=kLoop, calls=%fused_computation.325 | loop fusion | bytes 32 | tf_op jit(solution)/shard_map/slice | solution.py:130
  33.0 1.0 %multiply_reduce_fusion = (f32[4,128]{1,0:T(4,128)S(1)}, f32[4,6,128]{2,0,1:T(4,128)S(1)}, f32[4,6,128]{2,0,1:T(4,128)S(1)}, f32[4,6,128]{2,0,1:T(4,128)S(1)}, f...) fusion(f32[4,6,128]{2,0,1:T(4,128)S(1)} %get-tuple-element.90, f32[6]{0:T(128)S(1)} %get-tuple-element.152, ...), kind=kLoop, calls=%fused_computation.254 | loop fusion | flops 340480 | bytes 86088 | tf_op jit(solution)/shard_map/reduce_sum | solution.py:208
  34.1 7.3 %collective-permute-start.4 = (f32[4,7,36,128]{3,0,2,1:T(4,128)S(1)}, f32[4,7,36,128]{3,0,2,1:T(4,128)S(1)}, u32[]{:S(2)}, u32[]{:S(2)}) collective-permute-start(f32[4,7,36,128]{3,0,2,1:T(4,128)S(1)} %pad_maximum_fusion.2), channel_id=1, source_target_pairs={{0,64},{64,128},{128,192},{192,256},{256,320},{320,384},{384,448},... | collective-permute-start | bytes 1548296 | tf_op jit(solution)/shard_map/ppermute | solution.py:26
  42.2 0.7 slice_multiply_fusion.11
  43.4 0.7 slice_multiply_fusion.9
  44.5 0.7 slice_multiply_fusion.7
  53.6 3.0 %collective-permute-start.5 = (f32[4,7,36,128]{3,0,2,1:T(4,128)S(1)}, f32[4,7,36,128]{3,0,2,1:T(4,128)S(1)}, u32[]{:S(2)}, u32[]{:S(2)}) collective-permute-start(f32[4,7,36,128]{3,0,2,1:T(4,128)S(1)} %collective-permute-done.4), channel_id=1, source_target_pairs={{0,64},{64,128},{128,192},{192,256},{256,320},{320,384},{384,448},... | collective-permute-start | bytes 1548296 | tf_op jit(solution)/shard_map/ppermute | solution.py:26
  57.0 5.5 %collective-permute-done.5 = f32[4,7,36,128]{3,0,2,1:T(4,128)S(1)} collective-permute-done((f32[4,7,36,128]{3,0,2,1:T(4,128)S(1)}, f32[4,7,36,128]{3,0,2,1:T(4,128)S(1)}, u32[]{:S(2)}, u32[]{:S(2)}) %collective-permute-start.5) | collective-permute-done | bytes 516128 | tf_op jit(solution)/shard_map/ppermute | solution.py:26
  62.6 3.7 %collective-permute-start.6 = (f32[4,7,36,128]{3,0,2,1:T(4,128)S(1)}, f32[4,7,36,128]{3,0,2,1:T(4,128)S(1)}, u32[]{:S(2)}, u32[]{:S(2)}) collective-permute-start(f32[4,7,36,128]{3,0,2,1:T(4,128)S(1)} %collective-permute-done.5), channel_id=1, source_target_pairs={{0,64},{64,128},{128,192},{192,256},{256,320},{320,384},{384,448},... | collective-permute-start | bytes 1548296 | tf_op jit(solution)/shard_map/ppermute | solution.py:26
  66.6 5.7 %collective-permute-done.6 = f32[4,7,36,128]{3,0,2,1:T(4,128)S(1)} collective-permute-done((f32[4,7,36,128]{3,0,2,1:T(4,128)S(1)}, f32[4,7,36,128]{3,0,2,1:T(4,128)S(1)}, u32[]{:S(2)}, u32[]{:S(2)}) %collective-permute-start.6) | collective-permute-done | bytes 516128 | tf_op jit(solution)/shard_map/ppermute | solution.py:26
  72.3 3.7 %collective-permute-start.7 = (f32[4,7,36,128]{3,0,2,1:T(4,128)S(1)}, f32[4,7,36,128]{3,0,2,1:T(4,128)S(1)}, u32[]{:S(2)}, u32[]{:S(2)}) collective-permute-start(f32[4,7,36,128]{3,0,2,1:T(4,128)S(1)} %collective-permute-done.6), channel_id=1, source_target_pairs={{0,64},{64,128},{128,192},{192,256},{256,320},{320,384},{384,448},... | collective-permute-start | bytes 1548296 | tf_op jit(solution)/shard_map/ppermute | solution.py:26
  76.8 5.2 %collective-permute-done.7 = f32[4,7,36,128]{3,0,2,1:T(4,128)S(1)} collective-permute-done((f32[4,7,36,128]{3,0,2,1:T(4,128)S(1)}, f32[4,7,36,128]{3,0,2,1:T(4,128)S(1)}, u32[]{:S(2)}, u32[]{:S(2)}) %collective-permute-start.7) | collective-permute-done | bytes 516128 | tf_op jit(solution)/shard_map/ppermute | solution.py:26
  82.5 4.0 %collective-permute-done.10 = f32[4,7,36,128]{3,0,2,1:T(4,128)S(1)} collective-permute-done((f32[4,7,36,128]{3,0,2,1:T(4,128)S(1)}, f32[4,7,36,128]{3,0,2,1:T(4,128)S(1)}, u32[]{:S(2)}, u32[]{:S(2)}) %collective-permute-start.10) | collective-permute-done | bytes 516128 | tf_op jit(solution)/shard_map/ppermute | solution.py:28
  88.2 0.6 multiply_add_fusion
  88.8 3.9 %subtract_multiply_fusion = f32[4,14,36,128]{3,0,2,1:T(4,128)S(1)} fusion(s32[]{:T(128)S(6)} %select_n.230, s32[]{:T(128)S(6)} %select_n.229, f32[4,22,36,128]{3,0,2,1:T(4,128)S(1)} %pad_dynamic-slice_fusion.1, s32[]{:T(128)S(6)} %select_n.227, s32[]{:T(128)S(6)} %select_n.226, s32[]{:T(128)S(6)} %select_n.225, s32[]{:T(128)S(6)} %select_n.223, ...), kind=kLoop, calls=%fused_computation.28 | loop fusion | flops 5160960 | bytes 6193196 | tf_op jit(solution)/shard_map/mul | solution.py:143
  92.8 3.2 %fusion.93 = f32[4,6,36,128]{3,0,2,1:T(4,128)} fusion(f32[4,6,36,128]{3,0,2,1:T(4,128)S(1)} %get-tuple-element.91, f32[4,6,18,128]{3,0,2,1:T(4,128)S(1)} %get-tuple-element.129, f32[4,6,18,128]{3,0,2,1:T(4,128)S(1)} %get-tuple-element.128, f32[4,14,36,128]{3,0,2,1:T(4,128)S(1)} %subtract_multiply_fusion, s32[]{:T(128)S(6)} %select_n.238, s32[]{:T(128)S(6)} %select_n.237, ...), kind=kLoop, calls=%fused_computation.191 | loop fusion | flops 2211840 | bytes 2805800 | tf_op jit(solution)/shard_map/mul | solution.py:263
  (112 shorter events, 14.6 us)
Async XLA Ops:
  4.5 28.2 %collective-permute-start.2 = (f32[4,7,18,128]{3,0,2,1:T(4,128)S(1)}, f32[4,7,18,128]{3,0,2,1:T(4,128)S(1)}, u32[]{:S(2)}, u32[]{:S(2)}) collective-permute-start(f32[4,7,18,128]{3,0,2,1:T(4,128)S(1)} %get-tuple-element.123), channel_id=1, source_target_pairs={{1,0},{2,1},{3,2},{4,3},{5,4},{6,5},{7,6},{8,7},{9,8},{10,9},{11,1... | collective-permute-start | bytes 774152 | tf_op jit(solution)/shard_map/ppermute | solution.py:39
  5.8 27.0 %collective-permute-start.3 = (f32[4,7,18,128]{3,0,2,1:T(4,128)S(1)}, f32[4,7,18,128]{3,0,2,1:T(4,128)S(1)}, u32[]{:S(2)}, u32[]{:S(2)}) collective-permute-start(f32[4,7,18,128]{3,0,2,1:T(4,128)S(1)} %get-tuple-element.123), channel_id=1, source_target_pairs={{2,0},{3,1},{4,2},{5,3},{6,4},{7,5},{8,6},{9,7},{10,8},{11,9},{12,... | collective-permute-start | bytes 774152 | tf_op jit(solution)/shard_map/ppermute | solution.py:39
  7.1 25.6 %collective-permute-start = (f32[4,7,18,128]{3,0,2,1:T(4,128)S(1)}, f32[4,7,18,128]{3,0,2,1:T(4,128)S(1)}, u32[]{:S(2)}, u32[]{:S(2)}) collective-permute-start(f32[4,7,18,128]{3,0,2,1:T(4,128)S(1)} %get-tuple-element.122), channel_id=1, source_target_pairs={{0,1},{1,2},{2,3},{3,4},{4,5},{5,6},{6,7},{7,8},{8,9},{9,10},{10,1... | collective-permute-start | bytes 774152 | tf_op jit(solution)/shard_map/ppermute | solution.py:39
  11.1 21.7 %collective-permute-start.1 = (f32[4,7,18,128]{3,0,2,1:T(4,128)S(1)}, f32[4,7,18,128]{3,0,2,1:T(4,128)S(1)}, u32[]{:S(2)}, u32[]{:S(2)}) collective-permute-start(f32[4,7,18,128]{3,0,2,1:T(4,128)S(1)} %get-tuple-element.122), channel_id=1, source_target_pairs={{0,2},{1,3},{2,4},{3,5},{4,6},{5,7},{6,8},{7,9},{8,10},{9,11},{10,... | collective-permute-start | bytes 774152 | tf_op jit(solution)/shard_map/ppermute | solution.py:39
  34.1 19.4 %collective-permute-start.4 = (f32[4,7,36,128]{3,0,2,1:T(4,128)S(1)}, f32[4,7,36,128]{3,0,2,1:T(4,128)S(1)}, u32[]{:S(2)}, u32[]{:S(2)}) collective-permute-start(f32[4,7,36,128]{3,0,2,1:T(4,128)S(1)} %pad_maximum_fusion.2), channel_id=1, source_target_pairs={{0,64},{64,128},{128,192},{192,256},{256,320},{320,384},{384,448},... | collective-permute-start | bytes 1548296 | tf_op jit(solution)/shard_map/ppermute | solution.py:26
  41.4 25.2 %collective-permute-start.8 = (f32[4,7,36,128]{3,0,2,1:T(4,128)S(1)}, f32[4,7,36,128]{3,0,2,1:T(4,128)S(1)}, u32[]{:S(2)}, u32[]{:S(2)}) collective-permute-start(f32[4,7,36,128]{3,0,2,1:T(4,128)S(1)} %pad_maximum_fusion.2), channel_id=1, source_target_pairs={{0,448},{64,0},{128,64},{192,128},{256,192},{320,256},{384,320},{4... | collective-permute-start | bytes 1548296 | tf_op jit(solution)/shard_map/ppermute | solution.py:28
  53.6 9.0 %collective-permute-start.5 = (f32[4,7,36,128]{3,0,2,1:T(4,128)S(1)}, f32[4,7,36,128]{3,0,2,1:T(4,128)S(1)}, u32[]{:S(2)}, u32[]{:S(2)}) collective-permute-start(f32[4,7,36,128]{3,0,2,1:T(4,128)S(1)} %collective-permute-done.4), channel_id=1, source_target_pairs={{0,64},{64,128},{128,192},{192,256},{256,320},{320,384},{384,448},... | collective-permute-start | bytes 1548296 | tf_op jit(solution)/shard_map/ppermute | solution.py:26
  62.6 9.7 %collective-permute-start.6 = (f32[4,7,36,128]{3,0,2,1:T(4,128)S(1)}, f32[4,7,36,128]{3,0,2,1:T(4,128)S(1)}, u32[]{:S(2)}, u32[]{:S(2)}) collective-permute-start(f32[4,7,36,128]{3,0,2,1:T(4,128)S(1)} %collective-permute-done.5), channel_id=1, source_target_pairs={{0,64},{64,128},{128,192},{192,256},{256,320},{320,384},{384,448},... | collective-permute-start | bytes 1548296 | tf_op jit(solution)/shard_map/ppermute | solution.py:26
  66.6 10.2 %collective-permute-start.9 = (f32[4,7,36,128]{3,0,2,1:T(4,128)S(1)}, f32[4,7,36,128]{3,0,2,1:T(4,128)S(1)}, u32[]{:S(2)}, u32[]{:S(2)}) collective-permute-start(f32[4,7,36,128]{3,0,2,1:T(4,128)S(1)} %collective-permute-done.8), channel_id=1, source_target_pairs={{0,448},{64,0},{128,64},{192,128},{256,192},{320,256},{384,320},{4... | collective-permute-start | bytes 1548296 | tf_op jit(solution)/shard_map/ppermute | solution.py:28
  72.3 9.7 %collective-permute-start.7 = (f32[4,7,36,128]{3,0,2,1:T(4,128)S(1)}, f32[4,7,36,128]{3,0,2,1:T(4,128)S(1)}, u32[]{:S(2)}, u32[]{:S(2)}) collective-permute-start(f32[4,7,36,128]{3,0,2,1:T(4,128)S(1)} %collective-permute-done.6), channel_id=1, source_target_pairs={{0,64},{64,128},{128,192},{192,256},{256,320},{320,384},{384,448},... | collective-permute-start | bytes 1548296 | tf_op jit(solution)/shard_map/ppermute | solution.py:26
  76.8 9.7 %collective-permute-start.10 = (f32[4,7,36,128]{3,0,2,1:T(4,128)S(1)}, f32[4,7,36,128]{3,0,2,1:T(4,128)S(1)}, u32[]{:S(2)}, u32[]{:S(2)}) collective-permute-start(f32[4,7,36,128]{3,0,2,1:T(4,128)S(1)} %collective-permute-done.9), channel_id=1, source_target_pairs={{0,448},{64,0},{128,64},{192,128},{256,192},{320,256},{384,320},{4... | collective-permute-start | bytes 1548296 | tf_op jit(solution)/shard_map/ppermute | solution.py:28
  87.2 1.0 %copy-start = (s32[4,128]{1,0:T(4,128)S(1)}, s32[4,128]{1,0:T(4,128)}, u32[]{:S(2)}) copy-start(s32[4,128]{1,0:T(4,128)} %param.16) | copy-start | bytes 6148
  87.2 1.0 %copy-start.1 = (f32[4,128]{1,0:T(4,128)S(1)}, f32[4,128]{1,0:T(4,128)}, u32[]{:S(2)}) copy-start(f32[4,128]{1,0:T(4,128)} %param.17) | copy-start | bytes 6148
